TPU v7x, 512 devices: a whole 4x4x16 slice. The times are simulated.
512 devices in a mesh: dp: 4 (over z_hi, core), wide: 16 (over y, x), narrow: 8 (over z_lo).
Axes of the slice: x: 4, y: 4, z: 16 (z_hi: 2, z_lo: 8; z = z_hi * 8 + z_lo), core: 2. Of those that a mesh axis runs over, the one named last changes fastest.
Arguments:
- patches: bfloat16 [1024, 4, 6144], P('wide', 'dp'), parts along dimension 1, may hold values from -6 to 6
- vit_gain: float32 [6144], replicated, may hold values from 0.1 to 1.9
- vit_qkv: bfloat16 [6144, 3, 32, 128], P('narrow', None, 'wide'), may hold values from -4 to 4
- vit_in: bfloat16 [6144, 12288], P('narrow', 'wide'), may hold values from -0.078125 to 0.078125
- vit_attn_out: bfloat16 [4096, 6144], P('wide', 'narrow'), may hold values from -1 to 1
- vit_mlp_out: bfloat16 [12288, 6144], P('wide', 'narrow'), may hold values from -0.109375 to 0.109375
- proj: bfloat16 [6144, 4096], P('narrow', 'wide'), may hold values from -0.01953125 to 0.01953125
Outputs:
- encoded: bfloat16 [1024, 4, 4096], P('wide', 'dp', 'narrow'), parts along dimension 1
There are 4 independent parts, one for each index of `dp`. A program takes and returns all parts, laid end to end along the dimension named above; an argument that names none is the same for every part. Nothing has to cross between parts.
All inputs are finite; a program needn't handle non-finite values.
Results may differ from a plain program's by a relative error of at most 0.035.
Values may be sent and summed in bfloat16 or wider, within the bound.
No kernel may reach another device: no remote copies, remote signals or barrier semaphores. Data moves between devices by JAX's collectives and lax.ppermute only.
A program may use at most 64 MiB of HBM per device.

v0:
```python
import math
import jax
import jax.numpy as jnp
from jax import lax
from jax.sharding import PartitionSpec as P


def layer_norm(inputs, gain_row):
    widened = inputs.astype(jnp.float32)
    centred = widened - jnp.mean(widened, axis=-1, keepdims=True)
    variance = jnp.mean(centred * centred, axis=-1, keepdims=True)
    return (centred * lax.rsqrt(variance + 1e-06) * gain_row).astype(jnp.bfloat16)


def attend(queries, keys_all, values_all):
    score_scale = 1.0 / math.sqrt(queries.shape[-1])
    scores = (
        jnp.einsum("pihd,qihd->ihpq", queries, keys_all, preferred_element_type=jnp.float32)
        * score_scale
    )
    highest = jnp.max(scores, axis=-1, keepdims=True)
    exponentials = jnp.exp(scores - highest)
    totals = jnp.sum(exponentials, axis=-1)
    weights = exponentials.astype(jnp.bfloat16)
    mixed_sum = jnp.einsum(
        "ihpq,qihd->pihd", weights, values_all, preferred_element_type=jnp.float32
    )
    return (mixed_sum / jnp.transpose(totals, (2, 0, 1))[..., None]).astype(jnp.bfloat16)


def per_device(patches, vit_gain, vit_qkv, vit_in, vit_attn_out, vit_mlp_out, proj):
    local_rows = patches.shape[0]
    images = patches.shape[1]
    feature_block = vit_in.shape[0]
    heads_here = vit_qkv.shape[2]
    head_width = vit_qkv.shape[3]
    qkv_cols = 3 * heads_here * head_width
    narrow_start = lax.axis_index("narrow") * feature_block
    normed = layer_norm(patches, vit_gain)
    normed_part = lax.dynamic_slice_in_dim(normed, narrow_start, feature_block, 2)
    in_weight = jnp.concatenate([vit_qkv.reshape(feature_block, qkv_cols), vit_in], axis=1)
    piece_rows = lax.all_gather(normed_part, "wide", axis=0, tiled=True)
    flat_rows = piece_rows.reshape(-1, feature_block)
    joined = jnp.dot(flat_rows, in_weight, preferred_element_type=jnp.float32)
    partial_in = joined.reshape(piece_rows.shape[0], images, -1)
    summed_in = lax.psum(partial_in.astype(jnp.bfloat16), "narrow").astype(jnp.float32)
    row_count = summed_in.shape[0]
    qkv_all = (
        summed_in[..., :qkv_cols]
        .astype(jnp.bfloat16)
        .reshape(row_count, images, 3, heads_here, head_width)
    )
    activated = jax.nn.gelu(summed_in[..., qkv_cols:], approximate=False).astype(jnp.bfloat16)
    qkv_all, act_rows = (qkv_all, activated)
    mixed_heads = attend(qkv_all[:, :, 0], qkv_all[:, :, 1], qkv_all[:, :, 2])
    mixed_rows = mixed_heads.reshape(mixed_heads.shape[0], images, heads_here * head_width)
    heads_rows = mixed_rows.reshape(lax.axis_size("wide") * local_rows * images, -1)
    units_rows = act_rows.reshape(lax.axis_size("wide") * local_rows * images, -1)
    branch_terms = jnp.dot(heads_rows, vit_attn_out, preferred_element_type=jnp.float32)
    branch_terms = branch_terms + jnp.dot(
        units_rows, vit_mlp_out, preferred_element_type=jnp.float32
    )
    branch_sum = lax.psum_scatter(
        branch_terms.reshape(lax.axis_size("wide") * local_rows, images, -1).astype(jnp.bfloat16),
        "wide",
        scatter_dimension=0,
        tiled=True,
    ).astype(jnp.float32)
    own_columns = lax.dynamic_slice_in_dim(patches, narrow_start, feature_block, 2)
    vit_output = (own_columns.astype(jnp.float32) + branch_sum).astype(jnp.bfloat16)
    flat_output = vit_output.reshape(local_rows * images, feature_block)
    partial_encoded = jnp.dot(
        flat_output,
        lax.all_gather(proj, "wide", axis=1, tiled=True),
        preferred_element_type=jnp.float32,
    ).reshape(local_rows, images, -1)
    encoded = lax.psum_scatter(
        partial_encoded.astype(jnp.bfloat16), "narrow", scatter_dimension=2, tiled=True
    )
    return encoded


def solution(mesh):
    return jax.shard_map(
        per_device,
        mesh=mesh,
        in_specs=(
            P("wide", "dp", None),
            P(),
            P("narrow", None, "wide", None),
            P("narrow", "wide"),
            P("wide", "narrow"),
            P("wide", "narrow"),
            P("narrow", "wide"),
        ),
        out_specs=P("wide", "dp", "narrow"),
        check_vma=False,
    )
```

profile of v0, /device:TPU:4, one launch (start us, length us, event | category | flops | bytes accessed | tf_op | source)
XLA Modules:
  0.0 516.1 jit_solution(944441990527074840)
XLA Ops:
  6.5 0.0 copy-start
  6.5 0.0 all-gather.3.cloned.1.call-start
  6.5 1.4 convert_reduce_fusion
  8.0 1.5 multiply_reduce_fusion.1
  9.5 0.8 dynamic-slice
  10.3 0.7 fusion.86
  11.0 0.0 all-gather.3.cloned.1.call-update
  11.0 0.0 all-reduce.2.cloned.1.call-start
  11.1 3.1 reshape.76
  14.3 59.6 %all-gather.3.cloned.1.call-done = bf16[1024,1,768]{2,0,1:T(8,128)(2,1)} async-done(((bf16[64,1,768]{2,0,1:T(8,128)(2,1)}), bf16[1024,1,768]{2,0,1:T(8,128)(2,1)}) %all-gather.3.cloned.1.call-update) | async-done | bytes 1572880 | tf_op jit(solution)/shard_map/all_gather | solution.py:42
  73.9 6.0 %fusion.7 = bf16[1024,1,1536]{2,0,1:T(8,128)(2,1)} fusion(bf16[768,768]{1,0:T(8,128)(2,1)} %param.10, bf16[768,768]{1,0:T(8,128)(2,1)S(1)} %reshape.76, bf16[1024,1,768]{2,0,1:T(8,128)(2,1)} %all-gather.3.cloned.1.call-done), kind=kOutput, calls=%fused_computation.13 | convolution fusion | flops 2422210560 | bytes 7077888 | tf_op jit(solution)/shard_map/dot_general | solution.py:44
  79.9 0.0 all-reduce.2.cloned.1.call-update
  79.9 0.0 reduce-scatter.3.cloned.1.call-start
  80.0 166.4 %all-reduce.2.cloned.1.call-done = bf16[1024,1,1536]{2,0,1:T(8,128)(2,1)} async-done(((bf16[1024,1,1536]{2,0,1:T(8,128)(2,1)}), bf16[1024,1,1536]{2,0,1:T(8,128)(2,1)}) %all-reduce.2.cloned.1.call-update) | async-done | bytes 3145744 | tf_op jit(solution)/shard_map/psum | solution.py:46
  246.4 2.7 slice.25
  249.0 3.3 reshape.77
  252.4 2.1 fusion.123
  254.4 0.6 copy.13
  255.0 2.5 multiply_reduce_fusion
  257.5 1.4 fusion
  258.9 0.0 copy-start.1
  258.9 1.7 divide_convert_fusion
  260.6 0.0 copy-done
  260.6 0.2 copy-done.1
  260.8 0.0 copy-start.2
  260.8 7.8 %fusion.43 = f32[1024,768]{1,0:T(8,128)S(1)} fusion(bf16[768,768]{1,0:T(8,128)(2,1)S(1)} %copy-done, bf16[1024,1,1536]{2,0,1:T(8,128)(2,1)S(1)} %copy-done.1), kind=kOutput, calls=%fused_computation.52 | convolution fusion | flops 1259864064 | bytes 5898240 | tf_op jit(solution)/shard_map/dot_general | solution.py:60
  268.6 0.0 copy-done.2
  268.6 1.8 fusion.77
  270.4 0.0 reduce-scatter.3.cloned.1.call-update
  270.4 0.0 all-gather.5.cloned.1.call-start
  270.5 0.5 all-gather.5.cloned.1.call-update
  271.0 0.0 reduce-scatter.5.cloned.1.call-start
  271.1 84.1 %reduce-scatter.3.cloned.1.call-done = bf16[64,1,768]{2,0,1:T(8,128)(2,1)} async-done(((bf16[1024,1,768]{2,0,1:T(8,128)(2,1)}), bf16[64,1,768]{2,0,1:T(8,128)(2,1)}) %reduce-scatter.3.cloned.1.call-update) | async-done | bytes 98320 | tf_op jit(solution)/shard_map/reduce_scatter | solution.py:63
  355.1 83.4 %all-gather.5.cloned.1.call-done = bf16[768,4096]{1,0:T(8,128)(2,1)} async-done(((bf16[768,256]{1,0:T(8,128)(2,1)}), bf16[768,4096]{1,0:T(8,128)(2,1)}) %all-gather.5.cloned.1.call-update) | async-done | bytes 6291472 | tf_op jit(solution)/shard_map/all_gather | solution.py:74
  438.5 4.9 fusion.2
  443.4 0.0 reduce-scatter.5.cloned.1.call-update
  443.4 66.2 %reduce-scatter.5.cloned.1.call-done = bf16[64,1,512]{2,0,1:T(8,128)(2,1)} async-done(((bf16[64,1,4096]{2,0,1:T(8,128)(2,1)}), bf16[64,1,512]{2,0,1:T(8,128)(2,1)}) %reduce-scatter.5.cloned.1.call-update) | async-done | bytes 65552 | tf_op jit(solution)/shard_map/reduce_scatter | solution.py:77
  (2 shorter events, 0.0 us)
Async XLA Ops:
  6.5 254.0 %copy-start = (bf16[768,768]{1,0:T(8,128)(2,1)S(1)}, bf16[768,768]{1,0:T(8,128)(2,1)}, u32[]{:S(2)}) copy-start(bf16[768,768]{1,0:T(8,128)(2,1)} %param.12) | copy-start | bytes 3538948
  6.5 67.3 %all-gather.3.cloned.1.call-start = ((), (), s32[]{:S(2)}) async-start(), calls=%async_computation.2 | async-start | bytes 1671168 | tf_op jit(solution)/shard_map/all_gather | solution.py:42
  11.0 235.3 %all-reduce.2.cloned.1.call-start = ((), (), s32[]{:S(2)}) async-start(), calls=%async_computation.3 | async-start | bytes 6291456 | tf_op jit(solution)/shard_map/psum | solution.py:46
  79.9 275.2 %reduce-scatter.3.cloned.1.call-start = ((), (), s32[]{:S(2)}) async-start(), calls=%async_computation.4 | async-start | bytes 1671168 | tf_op jit(solution)/shard_map/reduce_scatter | solution.py:63
  258.9 1.9 copy-start.1
  260.8 7.8 %copy-start.2 = (bf16[256,768]{1,0:T(8,128)(2,1)S(1)}, bf16[256,768]{1,0:T(8,128)(2,1)}, u32[]{:S(2)}) copy-start(bf16[256,768]{1,0:T(8,128)(2,1)} %param.11) | copy-start | bytes 1179652
  270.4 168.0 %all-gather.5.cloned.1.call-start = ((), (), s32[]{:S(2)}) async-start(), calls=%async_computation.5 | async-start | bytes 6684672 | tf_op jit(solution)/shard_map/all_gather | solution.py:74
  271.0 238.6 %reduce-scatter.5.cloned.1.call-start = ((), (), s32[]{:S(2)}) async-start(), calls=%async_computation.6 | async-start | bytes 589824 | tf_op jit(solution)/shard_map/reduce_scatter | solution.py:77
Sparse Core Ops, SparseCore 0:
  11.2 62.6 all-gather.2
  80.0 166.2 all-reduce.1
  270.5 84.5 reduce-scatter.2
  358.0 80.4 all-gather.4
  443.5 66.0 reduce-scatter.4
where the time goes:
time: 517 us; the launch traced here: 516 us
  waiting for transfers between devices  460 us (89%)
  matrix products  24.7 us (5%)
  between operations  13.2 us (3%)
  local copies, waits for them, and re-layouts  12.8 us (2%)
    psum x1, waiting for transfers between devices, per_device(): lax.psum(partial_in.astype(jnp.bfloat16), 'narrow').astype(jnp.float32)  166 us
    reduce_scatter x1, waiting for transfers between devices, per_device(): lax.psum_scatter(branch_terms.reshape(lax.axis_size('wide') * local_rows,...  84.1 us
    all_gather x1, waiting for transfers between devices, per_device(): lax.all_gather(proj, 'wide', axis=1, tiled=True)  83.4 us
    reduce_scatter x1, waiting for transfers between devices, per_device(): lax.psum_scatter(partial_encoded.astype(jnp.bfloat16), 'narrow', scatter_...  66.2 us
    all_gather x1, waiting for transfers between devices, per_device(): piece_rows = lax.all_gather(normed_part, 'wide', axis=0, tiled=True)  59.6 us
  transfers between devices with their start and end apart: 5, of which 5 were waited for; matrix products, arithmetic and copies ran while one was open for 1% of the time, Pallas kernels for 0%

commit v1 on v0

--- a/solution.py
+++ b/solution.py
@@ -71,7 +71,9 @@
     flat_output = vit_output.reshape(local_rows * images, feature_block)
     partial_encoded = jnp.dot(
         flat_output,
-        lax.all_gather(proj, "wide", axis=1, tiled=True),
+        jnp.concatenate(
+            lax.all_to_all(jnp.stack([proj] * lax.axis_size("wide")), "wide", 0, 0), axis=1
+        ),
         preferred_element_type=jnp.float32,
     ).reshape(local_rows, images, -1)
     encoded = lax.psum_scatter(

time: 517 us -> 433 us (0.84)
  waiting for transfers between devices: 460 us -> 365 us
  starting transfers between devices: 0.17 us -> 6.3 us
    all_gather x1 -> x0, waiting for transfers between devices: 83.4 us -> none  [per_device(): lax.all_gather(proj, 'wide', axis=1, tiled=True)]
    psum x1, waiting for transfers between devices: 166 us -> 156 us  [per_device(): lax.psum(partial_in.astype(jnp.bfloat16), 'narrow').astype(jnp.float32)]
    all_to_all x0 -> x1, starting transfers between devices: none -> 6.18 us  [per_device(): lax.all_to_all(jnp.stack([proj] * lax.axis_size('wide')), 'wide', 0, 0)]
  transfers between devices with their start and end apart: 5 -> 5, of which waited for: 5 -> 4; matrix products, arithmetic and copies ran while one was open for 1% -> 7% of each run, Pallas kernels for 0% -> 0%
where the time goes in v1:
time: 433 us; the launch traced here: 432 us
  waiting for transfers between devices  365 us (84%)
  matrix products  25.5 us (6%)
  local copies, waits for them, and re-layouts  17.2 us (4%)
  between operations  13.2 us (3%)
  starting transfers between devices  6.3 us (1%)
  other arithmetic  5.06 us (1%)
    psum x1, waiting for transfers between devices, per_device(): lax.psum(partial_in.astype(jnp.bfloat16), 'narrow').astype(jnp.float32)  156 us
    reduce_scatter x1, waiting for transfers between devices, per_device(): lax.psum_scatter(branch_terms.reshape(lax.axis_size('wide') * local_rows,...  84.6 us
    reduce_scatter x1, waiting for transfers between devices, per_device(): lax.psum_scatter(partial_encoded.astype(jnp.bfloat16), 'narrow', scatter_...  65 us
    all_gather x1, waiting for transfers between devices, per_device(): piece_rows = lax.all_gather(normed_part, 'wide', axis=0, tiled=True)  59.6 us
  transfers between devices with their start and end apart: 5, of which 4 were waited for; matrix products, arithmetic and copies ran while one was open for 7% of the time, Pallas kernels for 0%

profile of v1, /device:TPU:4, one launch (start us, length us, event | category | flops | bytes accessed | tf_op | source)
XLA Modules:
  0.0 432.3 jit_solution(6975898468878738226)
XLA Ops:
  6.5 0.0 copy-start
  6.5 0.0 all-gather.2.cloned.1.call-start
  6.5 1.4 convert_reduce_fusion
  8.0 1.5 multiply_reduce_fusion.1
  9.5 0.8 dynamic-slice
  10.3 0.7 fusion.86
  11.0 0.0 all-gather.2.cloned.1.call-update
  11.0 0.0 all-reduce.2.cloned.1.call-start
  11.1 3.1 reshape.84
  14.3 59.6 %all-gather.2.cloned.1.call-done = bf16[1024,1,768]{2,0,1:T(8,128)(2,1)} async-done(((bf16[64,1,768]{2,0,1:T(8,128)(2,1)}), bf16[1024,1,768]{2,0,1:T(8,128)(2,1)}) %all-gather.2.cloned.1.call-update) | async-done | bytes 1572880 | tf_op jit(solution)/shard_map/all_gather | solution.py:42
  73.9 6.0 %fusion.7 = bf16[1024,1,1536]{2,0,1:T(8,128)(2,1)} fusion(bf16[768,768]{1,0:T(8,128)(2,1)} %param.10, bf16[768,768]{1,0:T(8,128)(2,1)S(1)} %reshape.84, bf16[1024,1,768]{2,0,1:T(8,128)(2,1)} %all-gather.2.cloned.1.call-done), kind=kOutput, calls=%fused_computation.13 | convolution fusion | flops 2422210560 | bytes 7077888 | tf_op jit(solution)/shard_map/dot_general | solution.py:44
  79.9 0.0 copy-start.2
  79.9 0.0 all-reduce.2.cloned.1.call-update
  79.9 1.0 copy-done.2
  80.9 0.2 copy.16
  81.0 3.3 stack.2
  84.3 6.2 %all-to-all-start = ((bf16[16,768,256]{1,2,0:T(8,128)(2,1)}), bf16[16,768,256]{1,2,0:T(8,128)(2,1)}, u32[]{:S(2)}, u32[]{:S(2)}) async-start(bf16[16,768,256]{1,2,0:T(8,128)(2,1)} %stack.2), calls=%async_computation.1 | async-start | bytes 12582912 | tf_op jit(solution)/shard_map/all_to_all | solution.py:75
  90.5 0.0 reduce-scatter.3.cloned.1.call-start
  90.5 155.8 %all-reduce.2.cloned.1.call-done = bf16[1024,1,1536]{2,0,1:T(8,128)(2,1)} async-done(((bf16[1024,1,1536]{2,0,1:T(8,128)(2,1)}), bf16[1024,1,1536]{2,0,1:T(8,128)(2,1)}) %all-reduce.2.cloned.1.call-update) | async-done | bytes 3145744 | tf_op jit(solution)/shard_map/psum | solution.py:46
  246.3 2.7 slice.25
  249.0 3.3 reshape.85
  252.3 2.1 fusion.123
  254.4 0.6 copy.18
  255.0 2.5 multiply_reduce_fusion
  257.5 1.4 fusion
  258.8 0.0 copy-start.1
  258.9 1.7 divide_convert_fusion
  260.5 0.0 copy-done
  260.5 0.2 copy-done.1
  260.7 0.0 copy-start.3
  260.7 7.8 %fusion.43 = f32[1024,768]{1,0:T(8,128)S(1)} fusion(bf16[768,768]{1,0:T(8,128)(2,1)S(1)} %copy-done, bf16[1024,1,1536]{2,0,1:T(8,128)(2,1)S(1)} %copy-done.1), kind=kOutput, calls=%fused_computation.52 | convolution fusion | flops 1259864064 | bytes 5898240 | tf_op jit(solution)/shard_map/dot_general | solution.py:60
  268.6 0.0 copy-done.3
  268.6 1.8 fusion.77
  270.4 0.0 reduce-scatter.3.cloned.1.call-update
  270.4 0.0 reduce-scatter.5.cloned.1.call-start
  270.5 0.0 all-to-all-done
  270.5 84.6 %reduce-scatter.3.cloned.1.call-done = bf16[64,1,768]{2,0,1:T(8,128)(2,1)} async-done(((bf16[1024,1,768]{2,0,1:T(8,128)(2,1)}), bf16[64,1,768]{2,0,1:T(8,128)(2,1)}) %reduce-scatter.3.cloned.1.call-update) | async-done | bytes 98320 | tf_op jit(solution)/shard_map/reduce_scatter | solution.py:63
  355.1 5.7 %fusion.2 = bf16[64,1,4096]{2,0,1:T(8,128)(2,1)} fusion(bf16[768,4096]{0,1:T(8,128)(2,1)} %bitcast.15, bf16[64,1,768]{2,0,1:T(8,128)(2,1)} %reduce-scatter.3.cloned.1.call-done, bf16[64,1,6144]{2,0,1:T(8,128)(2,1)} %param.7, s32[]{:T(128)S(6)} %select_n.4), kind=kOutput, calls=%fused_computation.6 | convolution fusion | flops 403111936 | bytes 7012356 | tf_op jit(solution)/shard_map/dot_general | solution.py:72
  360.8 0.0 reduce-scatter.5.cloned.1.call-update
  360.8 65.0 %reduce-scatter.5.cloned.1.call-done = bf16[64,1,512]{2,0,1:T(8,128)(2,1)} async-done(((bf16[64,1,4096]{2,0,1:T(8,128)(2,1)}), bf16[64,1,512]{2,0,1:T(8,128)(2,1)}) %reduce-scatter.5.cloned.1.call-update) | async-done | bytes 65552 | tf_op jit(solution)/shard_map/reduce_scatter | solution.py:79
  (2 shorter events, 0.0 us)
Async XLA Ops:
  6.5 254.0 %copy-start = (bf16[768,768]{1,0:T(8,128)(2,1)S(1)}, bf16[768,768]{1,0:T(8,128)(2,1)}, u32[]{:S(2)}) copy-start(bf16[768,768]{1,0:T(8,128)(2,1)} %param.12) | copy-start | bytes 3538948
  6.5 67.3 %all-gather.2.cloned.1.call-start = ((), (), s32[]{:S(2)}) async-start(), calls=%async_computation.3 | async-start | bytes 1671168 | tf_op jit(solution)/shard_map/all_gather | solution.py:42
  11.0 235.3 %all-reduce.2.cloned.1.call-start = ((), (), s32[]{:S(2)}) async-start(), calls=%async_computation.4 | async-start | bytes 6291456 | tf_op jit(solution)/shard_map/psum | solution.py:46
  79.9 1.0 copy-start.2
  84.3 186.2 %all-to-all-start = ((bf16[16,768,256]{1,2,0:T(8,128)(2,1)}), bf16[16,768,256]{1,2,0:T(8,128)(2,1)}, u32[]{:S(2)}, u32[]{:S(2)}) async-start(bf16[16,768,256]{1,2,0:T(8,128)(2,1)} %stack.2), calls=%async_computation.1 | async-start | bytes 12582912 | tf_op jit(solution)/shard_map/all_to_all | solution.py:75
  90.5 264.6 %reduce-scatter.3.cloned.1.call-start = ((), (), s32[]{:S(2)}) async-start(), calls=%async_computation.5 | async-start | bytes 1671168 | tf_op jit(solution)/shard_map/reduce_scatter | solution.py:63
  258.8 1.9 copy-start.1
  260.7 7.8 %copy-start.3 = (bf16[256,768]{1,0:T(8,128)(2,1)S(1)}, bf16[256,768]{1,0:T(8,128)(2,1)}, u32[]{:S(2)}) copy-start(bf16[256,768]{1,0:T(8,128)(2,1)} %param.11) | copy-start | bytes 1179652
  270.4 155.3 %reduce-scatter.5.cloned.1.call-start = ((), (), s32[]{:S(2)}) async-start(), calls=%async_computation.6 | async-start | bytes 589824 | tf_op jit(solution)/shard_map/reduce_scatter | solution.py:79
Sparse Core Ops, SparseCore 0:
  11.2 62.6 all-gather.1
  80.0 166.2 all-reduce.1
  270.6 84.4 reduce-scatter.2
  360.9 64.8 reduce-scatter.4

commit v2 on v0

--- a/solution.py
+++ b/solution.py
@@ -43,7 +43,9 @@
     flat_rows = piece_rows.reshape(-1, feature_block)
     joined = jnp.dot(flat_rows, in_weight, preferred_element_type=jnp.float32)
     partial_in = joined.reshape(piece_rows.shape[0], images, -1)
-    summed_in = lax.psum(partial_in.astype(jnp.bfloat16), "narrow").astype(jnp.float32)
+    summed_in = jnp.sum(lax.all_gather(partial_in.astype(jnp.bfloat16), "narrow"), axis=0).astype(
+        jnp.float32
+    )
     row_count = summed_in.shape[0]
     qkv_all = (
         summed_in[..., :qkv_cols]

time: 517 us -> 827 us (1.60)
  waiting for transfers between devices: 460 us -> 760 us
  other arithmetic: 5.06 us -> 20.5 us
    all_gather x0 -> x1, waiting for transfers between devices: none -> 491 us  [per_device(): lax.all_gather(partial_in.astype(jnp.bfloat16), 'narrow')]
    psum x1 -> x0, waiting for transfers between devices: 166 us -> none  [per_device(): lax.psum(partial_in.astype(jnp.bfloat16), 'narrow').astype(jnp.float32)]
    all_gather x1, waiting for transfers between devices: 83.4 us -> 49.8 us  [per_device(): lax.all_gather(proj, 'wide', axis=1, tiled=True)]
    reduce_sum x0 -> x1, other arithmetic: none -> 15.4 us  [per_device(): jnp.sum(lax.all_gather(partial_in.astype(jnp.bfloat16), 'narrow'), axis=0)]
    reduce_scatter x1, waiting for transfers between devices: 84.1 us -> 94.5 us  [per_device(): lax.psum_scatter(branch_terms.reshape(lax.axis_size('wide') * local_rows,...]
  transfers between devices with their start and end apart: 5 -> 5, of which waited for: 5 -> 5; matrix products, arithmetic and copies ran while one was open for 1% -> 5% of each run, Pallas kernels for 0% -> 0%
where the time goes in v2:
time: 827 us
  waiting for transfers between devices  760 us (92%)
  matrix products  25.9 us (3%)
  other arithmetic  20.5 us (2%)
  between operations  13.2 us (2%)
    all_gather x1, waiting for transfers between devices, per_device(): lax.all_gather(partial_in.astype(jnp.bfloat16), 'narrow')  491 us
    reduce_scatter x1, waiting for transfers between devices, per_device(): lax.psum_scatter(branch_terms.reshape(lax.axis_size('wide') * local_rows,...  94.5 us
    reduce_scatter x1, waiting for transfers between devices, per_device(): lax.psum_scatter(partial_encoded.astype(jnp.bfloat16), 'narrow', scatter_...  65 us
    all_gather x1, waiting for transfers between devices, per_device(): piece_rows = lax.all_gather(normed_part, 'wide', axis=0, tiled=True)  59.6 us
    all_gather x1, waiting for transfers between devices, per_device(): lax.all_gather(proj, 'wide', axis=1, tiled=True)  49.8 us
  transfers between devices with their start and end apart: 5, of which 5 were waited for; matrix products, arithmetic and copies ran while one was open for 5% of the time, Pallas kernels for 0%

profile of v2, /device:TPU:4, one launch (start us, length us, event | category | flops | bytes accessed | tf_op | source)
XLA Modules:
  0.0 827.1 jit_solution(14936712825952552760)
XLA Ops:
  6.5 0.0 copy-start
  6.5 0.0 all-gather.5.cloned.1.call-start
  6.5 1.4 convert_reduce_fusion
  8.0 1.5 multiply_reduce_fusion.1
  9.5 0.8 dynamic-slice
  10.3 0.7 fusion.84
  11.0 0.0 all-gather.5.cloned.1.call-update
  11.0 0.0 all-gather.9.cloned.1.call-start
  11.1 3.1 reshape.88
  14.2 59.6 %all-gather.5.cloned.1.call-done = bf16[1024,1,768]{2,0,1:T(8,128)(2,1)} async-done(((bf16[64,1,768]{2,0,1:T(8,128)(2,1)}), bf16[1024,1,768]{2,0,1:T(8,128)(2,1)}) %all-gather.5.cloned.1.call-update) | async-done | bytes 1572880 | tf_op jit(solution)/shard_map/all_gather | solution.py:42
  73.8 6.0 convolution_convert_fusion.1
  79.8 0.0 all-gather.9.cloned.1.call-update
  79.8 0.0 all-gather.7.cloned.1.call-start
  79.9 0.7 all-gather.7.cloned.1.call-update
  80.6 0.0 reduce-scatter.3.cloned.1.call-start
  80.6 490.6 %all-gather.9.cloned.1.call-done = bf16[8192,1536]{1,0:T(8,128)(2,1)} async-done(((bf16[1024,1536]{1,0:T(8,128)(2,1)}), bf16[8192,1536]{1,0:T(8,128)(2,1)}) %all-gather.9.cloned.1.call-update) | async-done | bytes 25165840 | tf_op jit(solution)/shard_map/all_gather | solution.py:46
  571.2 15.4 %reduce.8 = bf16[1024,1536]{1,0:T(8,128)(2,1)} reduce(bf16[8,1024,1536]{2,1,0:T(8,128)(2,1)} %bitcast.47, bf16[]{:T(256)} %constant.10.clone.1), dimensions={0}, to_apply=%region_2.0 | reduce | flops 11010048 | bytes 28311554 | tf_op jit(solution)/shard_map/reduce_sum | solution.py:46
  586.7 1.5 slice.25
  588.2 1.7 copy.13
  589.8 2.5 multiply_reduce_fusion
  592.3 1.4 fusion
  593.7 0.0 copy-start.1
  593.7 2.9 divide_convert_fusion
  596.6 0.0 copy-done
  596.6 0.0 copy-done.1
  596.6 0.0 copy-start.2
  596.7 7.8 fusion.42
  604.5 0.0 copy-done.2
  604.5 1.8 fusion.76
  606.3 0.0 reduce-scatter.3.cloned.1.call-update
  606.3 0.0 reduce-scatter.5.cloned.1.call-start
  606.4 49.8 %all-gather.7.cloned.1.call-done = bf16[768,4096]{1,0:T(8,128)(2,1)} async-done(((bf16[768,256]{1,0:T(8,128)(2,1)}), bf16[768,4096]{1,0:T(8,128)(2,1)}) %all-gather.7.cloned.1.call-update) | async-done | bytes 6291472 | tf_op jit(solution)/shard_map/all_gather | solution.py:76
  656.1 94.5 %reduce-scatter.3.cloned.1.call-done = bf16[64,1,768]{2,0,1:T(8,128)(2,1)} async-done(((bf16[1024,1,768]{2,0,1:T(8,128)(2,1)}), bf16[64,1,768]{2,0,1:T(8,128)(2,1)}) %reduce-scatter.3.cloned.1.call-update) | async-done | bytes 98320 | tf_op jit(solution)/shard_map/reduce_scatter | solution.py:65
  750.6 4.9 fusion.2
  755.5 0.0 reduce-scatter.5.cloned.1.call-update
  755.6 65.0 %reduce-scatter.5.cloned.1.call-done = bf16[64,1,512]{2,0,1:T(8,128)(2,1)} async-done(((bf16[64,1,4096]{2,0,1:T(8,128)(2,1)}), bf16[64,1,512]{2,0,1:T(8,128)(2,1)}) %reduce-scatter.5.cloned.1.call-update) | async-done | bytes 65552 | tf_op jit(solution)/shard_map/reduce_scatter | solution.py:79
  (2 shorter events, 0.0 us)
Async XLA Ops:
  6.5 590.1 %copy-start = (bf16[768,768]{1,0:T(8,128)(2,1)S(1)}, bf16[768,768]{1,0:T(8,128)(2,1)}, u32[]{:S(2)}) copy-start(bf16[768,768]{1,0:T(8,128)(2,1)} %param.12) | copy-start | bytes 3538948
  6.5 67.3 %all-gather.5.cloned.1.call-start = ((), (), s32[]{:S(2)}) async-start(), calls=%async_computation.2 | async-start | bytes 1671168 | tf_op jit(solution)/shard_map/all_gather | solution.py:42
  11.0 560.2 %all-gather.9.cloned.1.call-start = ((), (), s32[]{:S(2)}) async-start(), calls=%async_computation.6 | async-start | bytes 28311552 | tf_op jit(solution)/shard_map/all_gather | solution.py:46
  79.8 576.3 %all-gather.7.cloned.1.call-start = ((), (), s32[]{:S(2)}) async-start(), calls=%async_computation.4 | async-start | bytes 6684672 | tf_op jit(solution)/shard_map/all_gather | solution.py:76
  80.6 670.0 %reduce-scatter.3.cloned.1.call-start = ((), (), s32[]{:S(2)}) async-start(), calls=%async_computation.3 | async-start | bytes 1671168 | tf_op jit(solution)/shard_map/reduce_scatter | solution.py:65
  593.7 2.9 copy-start.1
  596.6 7.9 copy-start.2
  606.3 214.3 %reduce-scatter.5.cloned.1.call-start = ((), (), s32[]{:S(2)}) async-start(), calls=%async_computation.5 | async-start | bytes 589824 | tf_op jit(solution)/shard_map/reduce_scatter | solution.py:79
Sparse Core Ops, SparseCore 0:
  11.1 62.6 all-gather.4
  80.0 491.2 all-gather.8
  574.2 81.8 all-gather.6
  660.1 90.4 reduce-scatter.2
  755.7 64.8 reduce-scatter.4
